TPU v7x, 32 devices: a whole 2x2x4 slice. The times are simulated.
32 devices in a mesh: row: 8 (over z, y), col: 4 (over x, core).
Axes of the slice: x: 2, y: 2, z: 4, core: 2. Of those that a mesh axis runs over, the one named last changes fastest.
Arguments:
- gram: float32 [16384, 16384], P('row', 'col'), may hold values from -1 to 17, as said below
Outputs:
- factored: float32 [16384, 16384], P('row', 'col')
Inputs may be any that keep to these rules, and one draw needn't show every extreme that they name: gram holds a symmetric positive definite matrix in the block-cyclic order of the steps.
All inputs are finite; a program needn't handle non-finite values.
Results may differ from a plain program's by a relative error of at most 0.0001.
Values sent between devices are 32-bit elements; how exact they have to be, the bound alone decides.
No kernel may reach another device: no remote copies, remote signals or barrier semaphores. Data moves between devices by JAX's collectives and lax.ppermute only.
A program may use at most 192 MiB of HBM per device.

v0:
```python
import jax
import jax.numpy as jnp
from jax import lax
from jax.sharding import PartitionSpec as P

NB = 512
STEPS = 2


def broadcast(value, axis, source):
    kept = jnp.where(lax.axis_index(axis) == source, value, 0).astype(value.dtype)
    return lax.psum(kept, axis)


def from_partner(block, axis, apart):
    count = lax.axis_size(axis)
    route = []
    for low in range(count):
        high = low | 1 << apart
        if high != low and high < count:
            route += [(low, high), (high, low)]
    return lax.ppermute(block, axis, route)


def global_index(count, block, grid, position):
    ladder = jnp.arange(count, dtype=jnp.int32)
    return (ladder // block * grid + position) * block + ladder % block


def times_transposed(left, right):
    return lax.dot_general(
        left,
        right,
        (((1,), (1,)), ((), ())),
        precision=lax.Precision.HIGHEST,
        preferred_element_type=jnp.float32,
    )


def local(gram):
    grid_rows = lax.axis_size("row")
    grid_cols = lax.axis_size("col")
    row_id = lax.axis_index("row")
    col_id = lax.axis_index("col")
    rblock = NB * grid_cols // grid_rows
    per_class = grid_rows // grid_cols
    local_rows = gram.shape[0]
    local_cols = gram.shape[1]
    blocks = local_rows // rblock
    grows = global_index(local_rows, rblock, grid_rows, row_id)
    gcols = global_index(local_cols, NB, grid_cols, col_id)
    member = row_id % per_class
    row_class = row_id // per_class
    identity = jnp.eye(NB, dtype=jnp.float32)

    def factor_panel(matrix, panel_index):
        owner_col = panel_index % grid_cols
        local_block = panel_index // grid_cols
        end_row = panel_index * NB + NB
        column = matrix[:, local_block * NB : (local_block + 1) * NB]
        square = column[local_block * rblock : (local_block + 1) * rblock]
        is_owner = col_id == owner_col
        in_class = row_class == owner_col
        select = (jnp.arange(per_class, dtype=jnp.int32) == member).astype(jnp.float32)
        weight = jnp.where(is_owner & in_class, 1.0, 0.0).astype(jnp.float32)
        placed = (select[:, None, None] * square[None]).reshape(NB, NB) * weight
        diagonal = lax.psum(placed, "row")
        diagonal = jnp.where(is_owner, diagonal, identity)
        low_factor = jnp.linalg.cholesky(diagonal)
        inverse = jax.scipy.linalg.solve_triangular(low_factor, identity, lower=True)
        solved = times_transposed(column, inverse)
        trailing = jnp.where((grows >= end_row)[:, None], solved, 0.0)
        rows_diag = lax.dynamic_slice_in_dim(low_factor, member * rblock, rblock, 0)
        previous = trailing[local_block * rblock : (local_block + 1) * rblock]
        patched = jnp.where(in_class, rows_diag, previous)
        factored = trailing.at[local_block * rblock : (local_block + 1) * rblock].set(patched)
        new_column = jnp.where(is_owner, factored, column)
        matrix = matrix.at[:, local_block * NB : (local_block + 1) * NB].set(new_column)
        return (matrix, trailing)

    matrix = gram
    for panel_index in range(STEPS):
        matrix, trailing = factor_panel(matrix, panel_index)
        spread_owner_col = panel_index % grid_cols
        spread_rows_all = broadcast(trailing, "col", spread_owner_col)
        pieces = spread_rows_all.reshape(grid_cols, blocks // grid_cols * rblock, NB)
        shift_bits = per_class.bit_length() - 1
        for bit_level in reversed(range(grid_cols.bit_length() - 1)):
            halfway = pieces.shape[0] // 2
            own_bit = row_class >> bit_level & 1
            wanted = col_id >> bit_level & 1
            upper = own_bit == 1
            retained = jnp.where(upper, pieces[halfway:], pieces[:halfway])
            outgoing = jnp.where(upper, pieces[:halfway], pieces[halfway:])
            received = from_partner(outgoing, "row", shift_bits + bit_level)
            pieces = jnp.where(own_bit == wanted, retained, received)
        gathered = lax.all_gather(pieces[0], "row", axis=0, tiled=True)
        spread_columns = gathered.reshape(grid_cols, per_class, blocks // grid_cols, rblock, NB)
        spread_columns = jnp.transpose(spread_columns, (0, 2, 1, 3, 4)).reshape(local_cols, NB)
        first_row = panel_index * NB
        apply_end_row = first_row + NB
        current = matrix
        updated = current - times_transposed(spread_rows_all, spread_columns)
        panel_rows = (grows >= first_row) & (grows < apply_end_row)
        beyond = gcols >= apply_end_row
        updated = jnp.where(panel_rows[:, None] & beyond[None, :], 0.0, updated)
        matrix = matrix.at[:, 0:local_cols].set(updated)
    matrix, trailing = factor_panel(matrix, STEPS)
    return matrix


def solution(mesh):
    placed = (P("row", "col"),)
    return jax.shard_map(
        local, mesh=mesh, in_specs=placed, out_specs=P("row", "col"), check_vma=False
    )
```

profile of v0, /device:TPU:0, one launch (start us, length us, event | category | flops | bytes accessed | tf_op | source)
XLA Modules:
  0.0 1543.9 jit_solution(489001765417519902)
XLA Ops:
  6.5 23.0 %copy.106 = f32[2048,4096]{1,0:T(8,128)} copy(f32[2048,4096]{1,0:T(8,128)} %param.24) | data formatting | bytes 67108864
  32.8 81.1 %all-reduce.7.cloned.1.call-done = f32[512,512]{0,1:T(8,128)} async-done(((f32[512,512]{0,1:T(8,128)}), f32[512,512]{0,1:T(8,128)}) %all-reduce.7.cloned.1.call-update) | async-done | bytes 1048592 | tf_op jit(solution)/shard_map/psum | solution.py:67
  118.1 11.7 cholesky.374
  130.0 9.8 custom-call.31
  140.5 11.7 cholesky.393
  152.3 10.0 custom-call.32
  162.9 11.7 cholesky.414
  174.6 9.8 custom-call.33
  185.1 11.7 cholesky.431
  203.0 8.4 while.16
  211.4 39.3 %custom-call.34 = f32[4,128,128]{1,2,0:T(8,128)S(1)} custom-call(f32[4,128,128]{2,1,0:T(8,128)S(1)} %get-tuple-element.139), custom_call_target="InvertDiagBlocksLowerTriangular" | custom-call | tf_op jit(solution)/shard_map/jit(_solve_triangular)/triangular_solve | solution.py:70
  255.5 10.6 broadcast_select_fusion.1
  266.2 84.3 %all-reduce.9.cloned.1.call-done = f32[2048,512]{1,0:T(8,128)} async-done(((f32[2048,512]{1,0:T(8,128)}), f32[2048,512]{1,0:T(8,128)}) %all-reduce.9.cloned.1.call-update) | async-done | bytes 4194320 | tf_op jit(solution)/shard_map/psum | solution.py:12
  350.5 4.8 slice_select_fusion.2
  357.7 90.7 %collective-permute-done = f32[2,512,512]{2,1,0:T(8,128)S(1)} collective-permute-done((f32[2,512,512]{2,1,0:T(8,128)}, f32[2,512,512]{2,1,0:T(8,128)S(1)}, u32[]{:S(2)}, u32[]{:S(2)}) %collective-permute-start) | collective-permute-done | bytes 2097184 | tf_op jit(solution)/shard_map/ppermute | solution.py:22
  453.6 23.9 %collective-permute-done.1 = f32[1,512,512]{2,1,0:T(8,128)} collective-permute-done((f32[1,512,512]{2,1,0:T(8,128)}, f32[1,512,512]{2,1,0:T(8,128)}, u32[]{:S(2)}, u32[]{:S(2)}) %collective-permute-start.1) | collective-permute-done | bytes 1048608 | tf_op jit(solution)/shard_map/ppermute | solution.py:22
  482.2 7.1 fusion
  489.3 116.8 %all-gather.5.cloned.1.call-done = f32[1,4096,512]{2,1,0:T(8,128)} async-done(((f32[1,512,512]{2,1,0:T(8,128)}), f32[1,4096,512]{2,1,0:T(8,128)}) %all-gather.5.cloned.1.call-update) | async-done | bytes 8388624 | tf_op jit(solution)/shard_map/all_gather | solution.py:97
  610.7 60.7 %subtract_select_fusion.1 = f32[2048,4096]{1,0:T(8,128)} fusion(f32[2048,4096]{1,0:T(8,128)} %fusion, pred[4096]{0:T(1024)(128)(4,1)S(1)} %broadcast_compare_fusion.1, pred[2048]{0:T(1024)(128)(4,1)S(1)} %get-tuple-element.222, f32[2048,512]{1,0:T(8,128)S(1)} %copy-done, f32[4096,512]{1,0:T(8,128)S(1)} %bitcast.177), kind=kOutput, calls=%fused_computation.7 | convolution fusion | flops 51564773376 | bytes 79697920 | tf_op jit(solution)/shard_map/dot_general | solution.py:31
  674.6 76.4 %all-reduce.11.cloned.1.call-done = f32[512,512]{0,1:T(8,128)} async-done(((f32[512,512]{0,1:T(8,128)}), f32[512,512]{0,1:T(8,128)}) %all-reduce.11.cloned.1.call-update) | async-done | bytes 1048592 | tf_op jit(solution)/shard_map/psum | solution.py:67
  754.0 11.7 cholesky.446
  765.9 9.8 custom-call.35
  776.4 11.7 cholesky.465
  788.1 10.0 custom-call.36
  798.8 11.7 cholesky.486
  810.6 9.8 custom-call.37
  821.0 11.7 cholesky.503
  839.8 8.4 while.17
  848.2 39.3 %custom-call.38 = f32[4,128,128]{1,2,0:T(8,128)S(1)} custom-call(f32[4,128,128]{2,1,0:T(8,128)S(1)} %get-tuple-element.140), custom_call_target="InvertDiagBlocksLowerTriangular" | custom-call | tf_op jit(solution)/shard_map/jit(_solve_triangular)/triangular_solve | solution.py:70
  892.3 10.6 broadcast_select_fusion
  903.1 85.0 %all-reduce.13.cloned.1.call-done = f32[2048,512]{1,0:T(8,128)} async-done(((f32[2048,512]{1,0:T(8,128)}), f32[2048,512]{1,0:T(8,128)}) %all-reduce.13.cloned.1.call-update) | async-done | bytes 4194320 | tf_op jit(solution)/shard_map/psum | solution.py:12
  993.4 90.5 %collective-permute-done.2 = f32[2,512,512]{2,1,0:T(8,128)S(1)} collective-permute-done((f32[2,512,512]{2,1,0:T(8,128)S(1)}, f32[2,512,512]{2,1,0:T(8,128)S(1)}, u32[]{:S(2)}, u32[]{:S(2)}) %collective-permute-start.2) | collective-permute-done | bytes 2097184 | tf_op jit(solution)/shard_map/ppermute | solution.py:22
  1085.1 23.7 %collective-permute-done.3 = f32[1,512,512]{2,1,0:T(8,128)S(1)} collective-permute-done((f32[1,512,512]{2,1,0:T(8,128)S(1)}, f32[1,512,512]{2,1,0:T(8,128)S(1)}, u32[]{:S(2)}, u32[]{:S(2)}) %collective-permute-start.3) | collective-permute-done | bytes 1048608 | tf_op jit(solution)/shard_map/ppermute | solution.py:22
  1112.3 5.8 fusion.1
  1118.1 118.1 %all-gather.7.cloned.1.call-done = f32[1,4096,512]{2,1,0:T(8,128)} async-done(((f32[1,512,512]{2,1,0:T(8,128)}), f32[1,4096,512]{2,1,0:T(8,128)}) %all-gather.7.cloned.1.call-update) | async-done | bytes 8388624 | tf_op jit(solution)/shard_map/all_gather | solution.py:97
  1240.8 60.9 %subtract_select_fusion = f32[2048,4096]{1,0:T(8,128)} fusion(f32[2048,4096]{1,0:T(8,128)} %fusion.1, pred[4096]{0:T(1024)(128)(4,1)S(1)} %broadcast_compare_fusion, pred[2048]{0:T(1024)(128)(4,1)S(1)} %compare_and_fusion.1, f32[2048,512]{1,0:T(8,128)S(1)} %copy-done.1, f32[4096,512]{1,0:T(8,128)S(1)} %bitcast.178), kind=kOutput, calls=%fused_computation.6 | convolution fusion | flops 51564773376 | bytes 79697920 | tf_op jit(solution)/shard_map/dot_general | solution.py:31
  1304.6 76.6 %all-reduce.15.cloned.1.call-done = f32[512,512]{0,1:T(8,128)} async-done(((f32[512,512]{0,1:T(8,128)}), f32[512,512]{0,1:T(8,128)}) %all-reduce.15.cloned.1.call-update) | async-done | bytes 1048592 | tf_op jit(solution)/shard_map/psum | solution.py:67
  1384.3 11.7 cholesky.518
  1396.1 9.8 custom-call.39
  1406.6 11.7 cholesky.537
  1418.4 10.2 custom-call.40
  1429.3 11.7 cholesky.558
  1441.0 9.8 custom-call.41
  1451.4 11.9 cholesky.575
  1469.8 8.1 while.18
  1478.0 39.3 %custom-call.42 = f32[4,128,128]{1,2,0:T(8,128)S(1)} custom-call(f32[4,128,128]{2,1,0:T(8,128)S(1)} %get-tuple-element.141), custom_call_target="InvertDiagBlocksLowerTriangular" | custom-call | tf_op jit(solution)/shard_map/jit(_solve_triangular)/triangular_solve | solution.py:70
  1522.1 8.7 fusion.14
  1531.0 5.8 fusion.2
  (199 shorter events, 108.4 us)
Async XLA Ops:
  6.5 107.3 %all-reduce.7.cloned.1.call-start = ((), (), s32[]{:S(2)}) async-start(), calls=%async_computation | async-start | bytes 2097152 | tf_op jit(solution)/shard_map/psum | solution.py:67
  32.6 317.9 %all-reduce.9.cloned.1.call-start = ((), (), s32[]{:S(2)}) async-start(), calls=%async_computation.1 | async-start | bytes 8388608 | tf_op jit(solution)/shard_map/psum | solution.py:12
  113.9 2.8 copy-start.2
  266.2 340.0 %all-gather.5.cloned.1.call-start = ((), (), s32[]{:S(2)}) async-start(), calls=%async_computation.5 | async-start | bytes 9437184 | tf_op jit(solution)/shard_map/all_gather | solution.py:97
  355.3 93.1 %collective-permute-start = (f32[2,512,512]{2,1,0:T(8,128)}, f32[2,512,512]{2,1,0:T(8,128)S(1)}, u32[]{:S(2)}, u32[]{:S(2)}) collective-permute-start(f32[2,512,512]{2,1,0:T(8,128)} %bitcast.13), channel_id=1, source_target_pairs={{0,16},{16,0},{4,20},{20,4},{8,24},{24,8},{12,28},{28,12},{1,17},{... | collective-permute-start | bytes 6291464 | tf_op jit(solution)/shard_map/ppermute | solution.py:22
  448.4 1.3 copy-start.7
  453.0 24.5 %collective-permute-start.1 = (f32[1,512,512]{2,1,0:T(8,128)}, f32[1,512,512]{2,1,0:T(8,128)}, u32[]{:S(2)}, u32[]{:S(2)}) collective-permute-start(f32[1,512,512]{2,1,0:T(8,128)} %slice_select_fusion.5), channel_id=1, source_target_pairs={{0,8},{8,0},{4,12},{12,4},{16,24},{24,16},{20,28},{28,20},{1,9},{9... | collective-permute-start | bytes 3145736 | tf_op jit(solution)/shard_map/ppermute | solution.py:22
  478.9 272.1 %all-reduce.11.cloned.1.call-start = ((), (), s32[]{:S(2)}) async-start(), calls=%async_computation.2 | async-start | bytes 2097152 | tf_op jit(solution)/shard_map/psum | solution.py:67
  606.1 4.6 copy-start
  674.4 313.7 %all-reduce.13.cloned.1.call-start = ((), (), s32[]{:S(2)}) async-start(), calls=%async_computation.3 | async-start | bytes 8388608 | tf_op jit(solution)/shard_map/psum | solution.py:12
  751.0 1.5 copy-start.3
  902.9 333.3 %all-gather.7.cloned.1.call-start = ((), (), s32[]{:S(2)}) async-start(), calls=%async_computation.6 | async-start | bytes 9437184 | tf_op jit(solution)/shard_map/all_gather | solution.py:97
  990.9 93.0 %collective-permute-start.2 = (f32[2,512,512]{2,1,0:T(8,128)S(1)}, f32[2,512,512]{2,1,0:T(8,128)S(1)}, u32[]{:S(2)}, u32[]{:S(2)}) collective-permute-start(f32[2,512,512]{2,1,0:T(8,128)S(1)} %bitcast.189), channel_id=1, source_target_pairs={{0,16},{16,0},{4,20},{20,4},{8,24},{24,8},{12,28},{28,12},{1,17},{... | collective-permute-start | bytes 6291464 | tf_op jit(solution)/shard_map/ppermute | solution.py:22
  1084.3 26.0 %copy-start.5 = (f32[512,512]{1,0:T(8,128)S(1)}, f32[512,512]{1,0:T(8,128)}, u32[]{:S(2)}) copy-start(f32[512,512]{1,0:T(8,128)} %get-tuple-element.169) | copy-start | bytes 3145732
  1084.6 24.2 %collective-permute-start.3 = (f32[1,512,512]{2,1,0:T(8,128)S(1)}, f32[1,512,512]{2,1,0:T(8,128)S(1)}, u32[]{:S(2)}, u32[]{:S(2)}) collective-permute-start(f32[1,512,512]{2,1,0:T(8,128)S(1)} %slice_select_fusion.4), channel_id=1, source_target_pairs={{0,8},{8,0},{4,12},{12,4},{16,24},{24,16},{20,28},{28,20},{1,9},{9... | collective-permute-start | bytes 3145736 | tf_op jit(solution)/shard_map/ppermute | solution.py:22
  1110.2 271.1 %all-reduce.15.cloned.1.call-start = ((), (), s32[]{:S(2)}) async-start(), calls=%async_computation.4 | async-start | bytes 2097152 | tf_op jit(solution)/shard_map/psum | solution.py:67
  1236.2 4.6 copy-start.1
  1381.3 1.5 copy-start.4
  1522.1 8.7 copy-start.6
Sparse Core Ops, SparseCore 0:
  32.7 81.0 all-reduce.6
  266.3 84.1 all-reduce.8
  479.1 127.0 all-gather.4
  674.5 76.4 all-reduce.10
  903.0 85.0 all-reduce.12
  1110.3 125.8 all-gather.6
  1304.7 76.4 all-reduce.14
where the time goes:
time: 1550 us; the launch traced here: 1540 us
  waiting for transfers between devices  867 us (56%)
  other arithmetic  408 us (26%)
  matrix products  171 us (11%)
  local copies, waits for them, and re-layouts  67.9 us (4%)
  between operations  22.3 us (1%)
    another operation x44, other arithmetic, factor_panel(): low_factor = jnp.linalg.cholesky(diagonal)  238 us
    all_gather x2, waiting for transfers between devices, local(): gathered = lax.all_gather(pieces[0], 'row', axis=0, tiled=True)  235 us
    psum x3, waiting for transfers between devices, factor_panel(): diagonal = lax.psum(placed, 'row')  234 us
    ppermute x4, waiting for transfers between devices, from_partner(): return lax.ppermute(block, axis, route)  229 us
    psum x2, waiting for transfers between devices, broadcast(): return lax.psum(kept, axis)  169 us
    dot_general x5, matrix products, times_transposed(): lax.dot_general(left, right, (((1,), (1,)), ((), ())), precision=lax.Prec...  152 us
    another operation x7, other arithmetic, factor_panel(): jax.scipy.linalg.solve_triangular(low_factor, identity, lower=True)  122 us
  transfers between devices with their start and end apart: 11, of which 11 were waited for; matrix products, arithmetic and copies ran while one was open for 1% of the time, Pallas kernels for 0%

commit v1 on v0

--- a/solution.py
+++ b/solution.py
@@ -64,7 +64,11 @@
         select = (jnp.arange(per_class, dtype=jnp.int32) == member).astype(jnp.float32)
         weight = jnp.where(is_owner & in_class, 1.0, 0.0).astype(jnp.float32)
         placed = (select[:, None, None] * square[None]).reshape(NB, NB) * weight
-        diagonal = lax.psum(placed, "row")
+        diagonal = placed
+        for hop in (1, 2, 4):
+            diagonal = diagonal + lax.ppermute(
+                diagonal, "row", [(dev, dev ^ hop) for dev in range(8)]
+            )
         diagonal = jnp.where(is_owner, diagonal, identity)
         low_factor = jnp.linalg.cholesky(diagonal)
         inverse = jax.scipy.linalg.solve_triangular(low_factor, identity, lower=True)

time: 1550 us -> 1610 us (1.039)
  waiting for transfers between devices: 867 us -> 907 us
    ppermute x0 -> x9, waiting for transfers between devices: none -> 272 us  [factor_panel(): lax.ppermute(diagonal, 'row', [(dev, dev ^ hop) for dev in range(8)])]
    psum x3 -> x0, waiting for transfers between devices: 234 us -> none  [factor_panel(): diagonal = lax.psum(placed, 'row')]
  transfers between devices with their start and end apart: 11 -> 17, of which waited for: 11 -> 17; matrix products, arithmetic and copies ran while one was open for 1% -> 1% of each run, Pallas kernels for 0% -> 0%
where the time goes in v1:
time: 1610 us; the launch traced here: 1600 us
  waiting for transfers between devices  907 us (56%)
  other arithmetic  404 us (25%)
  matrix products  182 us (11%)
  local copies, waits for them, and re-layouts  67.7 us (4%)
  between operations  22.1 us (1%)
  starting transfers between devices  18.9 us (1%)
    ppermute x9, waiting for transfers between devices, factor_panel(): lax.ppermute(diagonal, 'row', [(dev, dev ^ hop) for dev in range(8)])  272 us
    another operation x44, other arithmetic, factor_panel(): low_factor = jnp.linalg.cholesky(diagonal)  238 us
    all_gather x2, waiting for transfers between devices, local(): gathered = lax.all_gather(pieces[0], 'row', axis=0, tiled=True)  235 us
    ppermute x4, waiting for transfers between devices, from_partner(): return lax.ppermute(block, axis, route)  229 us
    psum x2, waiting for transfers between devices, broadcast(): return lax.psum(kept, axis)  172 us
    dot_general x5, matrix products, times_transposed(): lax.dot_general(left, right, (((1,), (1,)), ((), ())), precision=lax.Prec...  152 us
    another operation x7, other arithmetic, factor_panel(): jax.scipy.linalg.solve_triangular(low_factor, identity, lower=True)  122 us
  transfers between devices with their start and end apart: 17, of which 17 were waited for; matrix products, arithmetic and copies ran while one was open for 1% of the time, Pallas kernels for 0%

profile of v1, /device:TPU:0, one launch (start us, length us, event | category | flops | bytes accessed | tf_op | source)
XLA Modules:
  0.0 1603.1 jit_solution(9918298096184406419)
XLA Ops:
  6.5 23.0 %copy.103 = f32[2048,4096]{1,0:T(8,128)} copy(f32[2048,4096]{1,0:T(8,128)} %param.24) | data formatting | bytes 67108864
  34.6 23.2 %collective-permute-done = f32[512,512]{0,1:T(8,128)S(1)} collective-permute-done((f32[512,512]{0,1:T(8,128)S(1)}, f32[512,512]{0,1:T(8,128)S(1)}, u32[]{:S(2)}, u32[]{:S(2)}) %collective-permute-start) | collective-permute-done | bytes 1048608 | tf_op jit(solution)/shard_map/ppermute | solution.py:69
  59.9 22.5 %collective-permute-done.1 = f32[512,512]{0,1:T(8,128)S(1)} collective-permute-done((f32[512,512]{0,1:T(8,128)S(1)}, f32[512,512]{0,1:T(8,128)S(1)}, u32[]{:S(2)}, u32[]{:S(2)}) %collective-permute-start.1) | collective-permute-done | bytes 1048608 | tf_op jit(solution)/shard_map/ppermute | solution.py:69
  85.3 44.3 %collective-permute-done.2 = f32[512,512]{0,1:T(8,128)} collective-permute-done((f32[512,512]{0,1:T(8,128)S(1)}, f32[512,512]{0,1:T(8,128)}, u32[]{:S(2)}, u32[]{:S(2)}) %collective-permute-start.2) | collective-permute-done | bytes 1048608 | tf_op jit(solution)/shard_map/ppermute | solution.py:69
  132.6 11.7 cholesky.374
  144.5 9.8 custom-call.31
  156.8 11.9 cholesky.393
  168.8 9.8 custom-call.32
  180.1 11.7 cholesky.414
  191.9 9.8 custom-call.33
  203.1 11.9 cholesky.431
  221.1 8.4 while.16
  229.5 39.3 %custom-call.34 = f32[4,128,128]{1,2,0:T(8,128)S(1)} custom-call(f32[4,128,128]{2,1,0:T(8,128)S(1)} %get-tuple-element.139), custom_call_target="InvertDiagBlocksLowerTriangular" | custom-call | tf_op jit(solution)/shard_map/jit(_solve_triangular)/triangular_solve | solution.py:74
  273.6 10.6 broadcast_select_fusion.1
  284.3 86.4 %all-reduce.4.cloned.1.call-done = f32[2048,512]{1,0:T(8,128)} async-done(((f32[2048,512]{1,0:T(8,128)}), f32[2048,512]{1,0:T(8,128)}) %all-reduce.4.cloned.1.call-update) | async-done | bytes 4194320 | tf_op jit(solution)/shard_map/psum | solution.py:12
  377.9 90.7 %collective-permute-done.3 = f32[2,512,512]{2,1,0:T(8,128)S(1)} collective-permute-done((f32[2,512,512]{2,1,0:T(8,128)}, f32[2,512,512]{2,1,0:T(8,128)S(1)}, u32[]{:S(2)}, u32[]{:S(2)}) %collective-permute-start.3) | collective-permute-done | bytes 2097184 | tf_op jit(solution)/shard_map/ppermute | solution.py:22
  473.8 23.9 %collective-permute-done.4 = f32[1,512,512]{2,1,0:T(8,128)} collective-permute-done((f32[1,512,512]{2,1,0:T(8,128)}, f32[1,512,512]{2,1,0:T(8,128)}, u32[]{:S(2)}, u32[]{:S(2)}) %collective-permute-start.4) | collective-permute-done | bytes 1048608 | tf_op jit(solution)/shard_map/ppermute | solution.py:22
  509.5 116.8 %all-gather.5.cloned.1.call-done = f32[1,4096,512]{2,1,0:T(8,128)} async-done(((f32[1,512,512]{2,1,0:T(8,128)}), f32[1,4096,512]{2,1,0:T(8,128)}) %all-gather.5.cloned.1.call-update) | async-done | bytes 8388624 | tf_op jit(solution)/shard_map/all_gather | solution.py:101
  630.9 60.9 %subtract_select_fusion.1 = f32[2048,4096]{1,0:T(8,128)} fusion(f32[2048,4096]{1,0:T(8,128)} %fusion, pred[4096]{0:T(1024)(128)(4,1)S(1)} %broadcast_compare_fusion.1, pred[2048]{0:T(1024)(128)(4,1)S(1)} %get-tuple-element.222, f32[2048,512]{1,0:T(8,128)S(1)} %copy-done, f32[4096,512]{1,0:T(8,128)S(1)} %bitcast.177), kind=kOutput, calls=%fused_computation.7 | convolution fusion | flops 51564773376 | bytes 79697920 | tf_op jit(solution)/shard_map/dot_general | solution.py:31
  694.3 23.6 %collective-permute-done.5 = f32[512,512]{0,1:T(8,128)S(1)} collective-permute-done((f32[512,512]{0,1:T(8,128)S(1)}, f32[512,512]{0,1:T(8,128)S(1)}, u32[]{:S(2)}, u32[]{:S(2)}) %collective-permute-start.5) | collective-permute-done | bytes 1048608 | tf_op jit(solution)/shard_map/ppermute | solution.py:69
  718.3 23.3 %collective-permute-done.6 = f32[512,512]{0,1:T(8,128)S(1)} collective-permute-done((f32[512,512]{0,1:T(8,128)S(1)}, f32[512,512]{0,1:T(8,128)S(1)}, u32[]{:S(2)}, u32[]{:S(2)}) %collective-permute-start.6) | collective-permute-done | bytes 1048608 | tf_op jit(solution)/shard_map/ppermute | solution.py:69
  743.7 44.1 %collective-permute-done.7 = f32[512,512]{0,1:T(8,128)} collective-permute-done((f32[512,512]{0,1:T(8,128)S(1)}, f32[512,512]{0,1:T(8,128)}, u32[]{:S(2)}, u32[]{:S(2)}) %collective-permute-start.7) | collective-permute-done | bytes 1048608 | tf_op jit(solution)/shard_map/ppermute | solution.py:69
  790.8 11.7 cholesky.446
  802.7 9.8 custom-call.35
  815.0 11.9 cholesky.465
  827.0 9.8 custom-call.36
  838.4 11.7 cholesky.486
  850.1 9.8 custom-call.37
  861.4 12.1 cholesky.503
  888.5 39.3 %custom-call.38 = f32[4,128,128]{1,2,0:T(8,128)S(1)} custom-call(f32[4,128,128]{2,1,0:T(8,128)S(1)} %get-tuple-element.140), custom_call_target="InvertDiagBlocksLowerTriangular" | custom-call | tf_op jit(solution)/shard_map/jit(_solve_triangular)/triangular_solve | solution.py:74
  932.7 10.8 broadcast_select_fusion
  943.5 85.4 %all-reduce.6.cloned.1.call-done = f32[2048,512]{1,0:T(8,128)} async-done(((f32[2048,512]{1,0:T(8,128)}), f32[2048,512]{1,0:T(8,128)}) %all-reduce.6.cloned.1.call-update) | async-done | bytes 4194320 | tf_op jit(solution)/shard_map/psum | solution.py:12
  1034.1 90.5 %collective-permute-done.8 = f32[2,512,512]{2,1,0:T(8,128)S(1)} collective-permute-done((f32[2,512,512]{2,1,0:T(8,128)S(1)}, f32[2,512,512]{2,1,0:T(8,128)S(1)}, u32[]{:S(2)}, u32[]{:S(2)}) %collective-permute-start.8) | collective-permute-done | bytes 2097184 | tf_op jit(solution)/shard_map/ppermute | solution.py:22
  1125.9 23.7 %collective-permute-done.9 = f32[1,512,512]{2,1,0:T(8,128)S(1)} collective-permute-done((f32[1,512,512]{2,1,0:T(8,128)S(1)}, f32[1,512,512]{2,1,0:T(8,128)S(1)}, u32[]{:S(2)}, u32[]{:S(2)}) %collective-permute-start.9) | collective-permute-done | bytes 1048608 | tf_op jit(solution)/shard_map/ppermute | solution.py:22
  1158.8 118.1 %all-gather.7.cloned.1.call-done = f32[1,4096,512]{2,1,0:T(8,128)} async-done(((f32[1,512,512]{2,1,0:T(8,128)}), f32[1,4096,512]{2,1,0:T(8,128)}) %all-gather.7.cloned.1.call-update) | async-done | bytes 8388624 | tf_op jit(solution)/shard_map/all_gather | solution.py:101
  1281.5 60.9 %subtract_select_fusion = f32[2048,4096]{1,0:T(8,128)} fusion(f32[2048,4096]{1,0:T(8,128)} %fusion.1, pred[4096]{0:T(1024)(128)(4,1)S(1)} %broadcast_compare_fusion, pred[2048]{0:T(1024)(128)(4,1)S(1)} %compare_and_fusion.1, f32[2048,512]{1,0:T(8,128)S(1)} %copy-done.1, f32[4096,512]{1,0:T(8,128)S(1)} %bitcast.178), kind=kOutput, calls=%fused_computation.6 | convolution fusion | flops 51564773376 | bytes 79697920 | tf_op jit(solution)/shard_map/dot_general | solution.py:31
  1344.9 23.6 %collective-permute-done.10 = f32[512,512]{0,1:T(8,128)S(1)} collective-permute-done((f32[512,512]{0,1:T(8,128)S(1)}, f32[512,512]{0,1:T(8,128)S(1)}, u32[]{:S(2)}, u32[]{:S(2)}) %collective-permute-start.10) | collective-permute-done | bytes 1048608 | tf_op jit(solution)/shard_map/ppermute | solution.py:69
  1368.9 23.3 %collective-permute-done.11 = f32[512,512]{0,1:T(8,128)S(1)} collective-permute-done((f32[512,512]{0,1:T(8,128)S(1)}, f32[512,512]{0,1:T(8,128)S(1)}, u32[]{:S(2)}, u32[]{:S(2)}) %collective-permute-start.11) | collective-permute-done | bytes 1048608 | tf_op jit(solution)/shard_map/ppermute | solution.py:69
  1394.3 44.0 %collective-permute-done.12 = f32[512,512]{0,1:T(8,128)S(1)} collective-permute-done((f32[512,512]{0,1:T(8,128)S(1)}, f32[512,512]{0,1:T(8,128)S(1)}, u32[]{:S(2)}, u32[]{:S(2)}) %collective-permute-start.12) | collective-permute-done | bytes 1048608 | tf_op jit(solution)/shard_map/ppermute | solution.py:69
  1440.1 11.7 cholesky.518
  1452.0 9.8 custom-call.39
  1464.4 12.2 cholesky.537
  1476.6 9.8 custom-call.40
  1488.0 11.7 cholesky.558
  1499.7 9.8 custom-call.41
  1511.0 11.9 cholesky.575
  1537.5 39.3 %custom-call.42 = f32[4,128,128]{1,2,0:T(8,128)S(1)} custom-call(f32[4,128,128]{2,1,0:T(8,128)S(1)} %get-tuple-element.141), custom_call_target="InvertDiagBlocksLowerTriangular" | custom-call | tf_op jit(solution)/shard_map/jit(_solve_triangular)/triangular_solve | solution.py:74
  1581.7 8.7 fusion.14
  (214 shorter events, 166.7 us)
Async XLA Ops:
  6.5 364.2 %all-reduce.4.cloned.1.call-start = ((), (), s32[]{:S(2)}) async-start(), calls=%async_computation | async-start | bytes 8388608 | tf_op jit(solution)/shard_map/psum | solution.py:12
  31.5 26.2 %collective-permute-start = (f32[512,512]{0,1:T(8,128)S(1)}, f32[512,512]{0,1:T(8,128)S(1)}, u32[]{:S(2)}, u32[]{:S(2)}) collective-permute-start(f32[512,512]{0,1:T(8,128)S(1)} %multiply_multiply_fusion.2), channel_id=1, source_target_pairs={{0,4},{4,0},{8,12},{12,8},{16,20},{20,16},{24,28},{28,24},{1,5},{5... | collective-permute-start | bytes 3145736 | tf_op jit(solution)/shard_map/ppermute | solution.py:69
  58.0 24.4 %collective-permute-start.1 = (f32[512,512]{0,1:T(8,128)S(1)}, f32[512,512]{0,1:T(8,128)S(1)}, u32[]{:S(2)}, u32[]{:S(2)}) collective-permute-start(f32[512,512]{0,1:T(8,128)S(1)} %fusion.186), channel_id=1, source_target_pairs={{0,8},{4,12},{8,0},{12,4},{16,24},{20,28},{24,16},{28,20},{1,9},{5... | collective-permute-start | bytes 3145736 | tf_op jit(solution)/shard_map/ppermute | solution.py:69
  82.6 47.0 %collective-permute-start.2 = (f32[512,512]{0,1:T(8,128)S(1)}, f32[512,512]{0,1:T(8,128)}, u32[]{:S(2)}, u32[]{:S(2)}) collective-permute-start(f32[512,512]{0,1:T(8,128)S(1)} %add.225), channel_id=1, source_target_pairs={{0,16},{4,20},{8,24},{12,28},{16,0},{20,4},{24,8},{28,12},{1,17},{... | collective-permute-start | bytes 3145736 | tf_op jit(solution)/shard_map/ppermute | solution.py:69
  131.6 1.0 copy-start.2
  284.3 342.1 %all-gather.5.cloned.1.call-start = ((), (), s32[]{:S(2)}) async-start(), calls=%async_computation.2 | async-start | bytes 9437184 | tf_op jit(solution)/shard_map/all_gather | solution.py:101
  375.5 93.1 %collective-permute-start.3 = (f32[2,512,512]{2,1,0:T(8,128)}, f32[2,512,512]{2,1,0:T(8,128)S(1)}, u32[]{:S(2)}, u32[]{:S(2)}) collective-permute-start(f32[2,512,512]{2,1,0:T(8,128)} %bitcast.13), channel_id=1, source_target_pairs={{0,16},{16,0},{4,20},{20,4},{8,24},{24,8},{12,28},{28,12},{1,17},{... | collective-permute-start | bytes 6291464 | tf_op jit(solution)/shard_map/ppermute | solution.py:22
  468.6 1.3 copy-start.7
  473.3 24.5 %collective-permute-start.4 = (f32[1,512,512]{2,1,0:T(8,128)}, f32[1,512,512]{2,1,0:T(8,128)}, u32[]{:S(2)}, u32[]{:S(2)}) collective-permute-start(f32[1,512,512]{2,1,0:T(8,128)} %slice_select_fusion.5), channel_id=1, source_target_pairs={{0,8},{8,0},{4,12},{12,4},{16,24},{24,16},{20,28},{28,20},{1,9},{9... | collective-permute-start | bytes 3145736 | tf_op jit(solution)/shard_map/ppermute | solution.py:22
  499.1 529.7 %all-reduce.6.cloned.1.call-start = ((), (), s32[]{:S(2)}) async-start(), calls=%async_computation.1 | async-start | bytes 8388608 | tf_op jit(solution)/shard_map/psum | solution.py:12
  626.3 4.6 copy-start
  693.7 24.2 %collective-permute-start.5 = (f32[512,512]{0,1:T(8,128)S(1)}, f32[512,512]{0,1:T(8,128)S(1)}, u32[]{:S(2)}, u32[]{:S(2)}) collective-permute-start(f32[512,512]{0,1:T(8,128)S(1)} %multiply_multiply_fusion.1), channel_id=1, source_target_pairs={{0,4},{4,0},{8,12},{12,8},{16,20},{20,16},{24,28},{28,24},{1,5},{5... | collective-permute-start | bytes 3145736 | tf_op jit(solution)/shard_map/ppermute | solution.py:69
  718.2 23.4 %collective-permute-start.6 = (f32[512,512]{0,1:T(8,128)S(1)}, f32[512,512]{0,1:T(8,128)S(1)}, u32[]{:S(2)}, u32[]{:S(2)}) collective-permute-start(f32[512,512]{0,1:T(8,128)S(1)} %fusion.185), channel_id=1, source_target_pairs={{0,8},{4,12},{8,0},{12,4},{16,24},{20,28},{24,16},{28,20},{1,9},{5... | collective-permute-start | bytes 3145736 | tf_op jit(solution)/shard_map/ppermute | solution.py:69
  741.8 46.0 %collective-permute-start.7 = (f32[512,512]{0,1:T(8,128)S(1)}, f32[512,512]{0,1:T(8,128)}, u32[]{:S(2)}, u32[]{:S(2)}) collective-permute-start(f32[512,512]{0,1:T(8,128)S(1)} %add.229), channel_id=1, source_target_pairs={{0,16},{4,20},{8,24},{12,28},{16,0},{20,4},{24,8},{28,12},{1,17},{... | collective-permute-start | bytes 3145736 | tf_op jit(solution)/shard_map/ppermute | solution.py:69
  789.8 1.0 copy-start.3
  943.4 333.5 %all-gather.7.cloned.1.call-start = ((), (), s32[]{:S(2)}) async-start(), calls=%async_computation.3 | async-start | bytes 9437184 | tf_op jit(solution)/shard_map/all_gather | solution.py:101
  1031.6 93.0 %collective-permute-start.8 = (f32[2,512,512]{2,1,0:T(8,128)S(1)}, f32[2,512,512]{2,1,0:T(8,128)S(1)}, u32[]{:S(2)}, u32[]{:S(2)}) collective-permute-start(f32[2,512,512]{2,1,0:T(8,128)S(1)} %bitcast.192), channel_id=1, source_target_pairs={{0,16},{16,0},{4,20},{20,4},{8,24},{24,8},{12,28},{28,12},{1,17},{... | collective-permute-start | bytes 6291464 | tf_op jit(solution)/shard_map/ppermute | solution.py:22
  1125.1 25.9 %copy-start.5 = (f32[512,512]{1,0:T(8,128)S(1)}, f32[512,512]{1,0:T(8,128)}, u32[]{:S(2)}) copy-start(f32[512,512]{1,0:T(8,128)} %get-tuple-element.169) | copy-start | bytes 3145732
  1125.3 24.2 %collective-permute-start.9 = (f32[1,512,512]{2,1,0:T(8,128)S(1)}, f32[1,512,512]{2,1,0:T(8,128)S(1)}, u32[]{:S(2)}, u32[]{:S(2)}) collective-permute-start(f32[1,512,512]{2,1,0:T(8,128)S(1)} %slice_select_fusion.4), channel_id=1, source_target_pairs={{0,8},{8,0},{4,12},{12,4},{16,24},{24,16},{20,28},{28,20},{1,9},{9... | collective-permute-start | bytes 3145736 | tf_op jit(solution)/shard_map/ppermute | solution.py:22
  1276.9 4.6 copy-start.1
  1344.3 24.3 %collective-permute-start.10 = (f32[512,512]{0,1:T(8,128)S(1)}, f32[512,512]{0,1:T(8,128)S(1)}, u32[]{:S(2)}, u32[]{:S(2)}) collective-permute-start(f32[512,512]{0,1:T(8,128)S(1)} %multiply_multiply_fusion), channel_id=1, source_target_pairs={{0,4},{4,0},{8,12},{12,8},{16,20},{20,16},{24,28},{28,24},{1,5},{5... | collective-permute-start | bytes 3145736 | tf_op jit(solution)/shard_map/ppermute | solution.py:69
  1368.8 23.4 %collective-permute-start.11 = (f32[512,512]{0,1:T(8,128)S(1)}, f32[512,512]{0,1:T(8,128)S(1)}, u32[]{:S(2)}, u32[]{:S(2)}) collective-permute-start(f32[512,512]{0,1:T(8,128)S(1)} %fusion.184), channel_id=1, source_target_pairs={{0,8},{4,12},{8,0},{12,4},{16,24},{20,28},{24,16},{28,20},{1,9},{5... | collective-permute-start | bytes 3145736 | tf_op jit(solution)/shard_map/ppermute | solution.py:69
  1392.4 45.9 %collective-permute-start.12 = (f32[512,512]{0,1:T(8,128)S(1)}, f32[512,512]{0,1:T(8,128)S(1)}, u32[]{:S(2)}, u32[]{:S(2)}) collective-permute-start(f32[512,512]{0,1:T(8,128)S(1)} %add.232), channel_id=1, source_target_pairs={{0,16},{4,20},{8,24},{12,28},{16,0},{20,4},{24,8},{28,12},{1,17},{... | collective-permute-start | bytes 3145736 | tf_op jit(solution)/shard_map/ppermute | solution.py:69
  1439.1 1.0 copy-start.4
  1581.6 8.7 copy-start.6
Sparse Core Ops, SparseCore 0:
  284.4 86.2 all-reduce.3
  499.3 127.0 all-gather.4
  943.6 85.2 all-reduce.5
  1151.1 125.8 all-gather.6
